TPU v7x, 32 devices: a whole 2x2x4 slice. The times are simulated.
32 devices in a mesh: tm: 8 (over z, y), col: 4 (over x, core).
Axes of the slice: x: 2, y: 2, z: 4, core: 2. Of those that a mesh axis runs over, the one named last changes fastest.
Arguments:
- observed: bfloat16 [16, 128, 512], P('tm', None, 'col'), may hold values from -6 to 6
- input_gain: float32 [512], P('col'), may hold values from 0.03 to 0.3
- persist: float32 [16, 512], P('tm', 'col'), may hold values from 0.5 to 1, as said below
- coupling: bfloat16 [16, 512, 512], P('tm', None, 'col'), may hold values from -0.02734375 to 0.02734375
- pattern: int32 [8, 8], replicated, may hold values 0 or 1
Outputs:
- filtered: float32 [16, 128, 512], P('tm', None, 'col')
- smoothed: float32 [16, 128, 512], P('tm', None, 'col')
Inputs may be any that keep to these rules, and one draw needn't show every extreme that they name: `persist`: persistence of each state component at each step.
All inputs are finite; a program needn't handle non-finite values.
Results may differ from a plain program's by a relative error of at most 0.0003.
Values may be sent and summed in bfloat16 or wider, within the bound.
No kernel may reach another device: no remote copies, remote signals or barrier semaphores. Data moves between devices by JAX's collectives and lax.ppermute only.
A program may use at most 64 MiB of HBM per device.

v0:
```python
import jax
import jax.numpy as jnp
from jax import lax
from jax.sharding import PartitionSpec as P


def passed_along(shard, axis, by):
    length = lax.axis_size(axis)
    pairs = [(i, i + by) for i in range(length) if 0 <= i + by < length]
    return lax.ppermute(shard, axis, pairs)


def split_dot(state, weights, transposed):
    high = state.astype(jnp.bfloat16)
    low = (state - high.astype(jnp.float32)).astype(jnp.bfloat16)
    both = jnp.concatenate([high, low], axis=0)
    contract = 1 if transposed else 0
    prod = lax.dot_general(
        both, weights, (((1,), (contract,)), ((), ())), preferred_element_type=jnp.float32
    )
    rows = state.shape[0]
    return prod[:rows] + prod[rows:]


def local(observed, input_gain, persist, coupling, pattern):
    step_count = observed.shape[0]
    state_width = coupling.shape[1]
    block_count = pattern.shape[0]
    block_size = state_width // block_count
    time_groups = lax.axis_size("tm")
    full_coupling = lax.all_gather(coupling, "col", axis=2, tiled=True)
    small = jnp.concatenate([persist, input_gain[None]], axis=0)
    small = lax.all_gather(small, "col", axis=1, tiled=True)
    diag = small[:step_count]
    gain = small[step_count]
    seen = lax.all_to_all(observed, "col", split_axis=1, concat_axis=2, tiled=True)
    mask = jnp.broadcast_to(
        pattern.astype(jnp.bfloat16)[:, None, :, None],
        (block_count, block_size, block_count, block_size),
    ).reshape(state_width, state_width)
    weights = full_coupling * mask[None]
    driven = gain[None, None, :] * seen.astype(jnp.float32)

    def forward(x):
        out = []
        for k in range(step_count):
            x = split_dot(x, weights[k], False) + x * diag[k][None] + driven[k]
            out.append(x)
        return out

    def backward(e):
        out = [None] * step_count
        out[step_count - 1] = e
        for k in range(step_count - 1, -1, -1):
            w = e + driven[k]
            e = split_dot(w, weights[k], True) + w * diag[k][None]
            if k > 0:
                out[k - 1] = e
        return (out, e)

    def stage(carry):
        x_in, e_in = carry
        xs = forward(x_in)
        _, e_out = backward(e_in)
        return (passed_along(xs[-1], "tm", 1), passed_along(e_out, "tm", -1))

    zeros = jnp.zeros(driven.shape[1:], jnp.float32)
    carry = (zeros, zeros)
    if time_groups <= 8:
        for _ in range(time_groups - 1):
            carry = stage(carry)
    else:
        carry = lax.fori_loop(0, time_groups - 1, lambda _, c: stage(c), carry)
    x_in, e_in = carry
    xs = forward(x_in)
    es, _ = backward(e_in)
    filtered = jnp.stack(xs)
    smoothed = jnp.stack([x + e for x, e in zip(xs, es)])
    both = jnp.stack([filtered, smoothed])
    both = lax.all_to_all(both, "col", split_axis=3, concat_axis=2, tiled=True)
    return (both[0], both[1])


def solution(mesh):
    return jax.shard_map(
        local,
        mesh=mesh,
        in_specs=(P("tm", None, "col"), P("col"), P("tm", "col"), P("tm", None, "col"), P()),
        out_specs=(P("tm", None, "col"), P("tm", None, "col")),
        check_vma=False,
    )
```

profile of v0, /device:TPU:0, one launch (start us, length us, event | category | flops | bytes accessed | tf_op | source)
XLA Modules:
  0.0 149.8 jit_solution(448652533752614488)
XLA Ops:
  8.7 4.2 %all-to-all-start = ((bf16[2,128,128]{2,0,1:T(2,128)(2,1)}), bf16[2,128,128]{2,0,1:T(2,128)(2,1)S(1)}, u32[]{:S(2)}, u32[]{:S(2)}) async-start(bf16[2,128,128]{2,0,1:T(2,128)(2,1)} %copy.10), calls=%async_computation | async-start | bytes 131072 | tf_op jit(solution)/shard_map/all_to_all | solution.py:36
  13.6 5.3 %all_gather.7 = f32[3,512]{1,0:T(4,128)S(1)} all-gather(f32[3,128]{1,0:T(4,128)S(1)} %pad_maximum_fusion.1), channel_id=1, replica_groups=mesh['tm'=8,'col'=4] {'col'}, dimensions={1}, use_global_device_ids=true | all-gather | bytes 7680 | tf_op jit(solution)/shard_map/all_gather | solution.py:33
  20.6 8.5 %all-gather.2.cloned.1.call-done = bf16[2,512,512]{2,1,0:T(8,128)(2,1)} async-done(((bf16[2,512,128]{2,1,0:T(8,128)(2,1)}), bf16[2,512,512]{2,1,0:T(8,128)(2,1)}) %all-gather.2.cloned.1.call-update) | async-done | bytes 1048592 | tf_op jit(solution)/shard_map/all_gather | solution.py:31
  29.1 1.3 broadcast_multiply_fusion
  30.9 3.4 %collective-permute-start = (f32[32,512]{1,0:T(8,128)S(1)}, f32[32,512]{1,0:T(8,128)S(1)}, u32[]{:S(2)}, u32[]{:S(2)}) collective-permute-start(f32[32,512]{1,0:T(8,128)S(1)} %fusion.53), channel_id=1, source_target_pairs={{0,4},{4,8},{8,12},{12,16},{16,20},{20,24},{24,28},{1,5},{5,9},{9,... | collective-permute-start | bytes 196616 | tf_op jit(solution)/shard_map/ppermute | solution.py:10
  34.3 1.9 %collective-permute-done = f32[32,512]{1,0:T(8,128)S(1)} collective-permute-done((f32[32,512]{1,0:T(8,128)S(1)}, f32[32,512]{1,0:T(8,128)S(1)}, u32[]{:S(2)}, u32[]{:S(2)}) %collective-permute-start) | collective-permute-done | bytes 65568 | tf_op jit(solution)/shard_map/ppermute | solution.py:10
  36.7 4.3 %collective-permute-start.1 = (f32[32,512]{1,0:T(8,128)S(1)}, f32[32,512]{1,0:T(8,128)S(1)}, u32[]{:S(2)}, u32[]{:S(2)}) collective-permute-start(f32[32,512]{1,0:T(8,128)S(1)} %fusion.49), channel_id=1, source_target_pairs={{0,4},{4,8},{8,12},{12,16},{16,20},{20,24},{24,28},{1,5},{5,9},{9,... | collective-permute-start | bytes 196616 | tf_op jit(solution)/shard_map/ppermute | solution.py:10
  40.9 1.9 %collective-permute-done.1 = f32[32,512]{1,0:T(8,128)S(1)} collective-permute-done((f32[32,512]{1,0:T(8,128)S(1)}, f32[32,512]{1,0:T(8,128)S(1)}, u32[]{:S(2)}, u32[]{:S(2)}) %collective-permute-start.1) | collective-permute-done | bytes 65568 | tf_op jit(solution)/shard_map/ppermute | solution.py:10
  43.3 4.3 %collective-permute-start.2 = (f32[32,512]{1,0:T(8,128)S(1)}, f32[32,512]{1,0:T(8,128)S(1)}, u32[]{:S(2)}, u32[]{:S(2)}) collective-permute-start(f32[32,512]{1,0:T(8,128)S(1)} %fusion.45), channel_id=1, source_target_pairs={{0,4},{4,8},{8,12},{12,16},{16,20},{20,24},{24,28},{1,5},{5,9},{9,... | collective-permute-start | bytes 196616 | tf_op jit(solution)/shard_map/ppermute | solution.py:10
  47.6 1.9 %collective-permute-done.2 = f32[32,512]{1,0:T(8,128)S(1)} collective-permute-done((f32[32,512]{1,0:T(8,128)S(1)}, f32[32,512]{1,0:T(8,128)S(1)}, u32[]{:S(2)}, u32[]{:S(2)}) %collective-permute-start.2) | collective-permute-done | bytes 65568 | tf_op jit(solution)/shard_map/ppermute | solution.py:10
  50.0 5.2 %collective-permute-start.3 = (f32[32,512]{1,0:T(8,128)S(1)}, f32[32,512]{1,0:T(8,128)S(1)}, u32[]{:S(2)}, u32[]{:S(2)}) collective-permute-start(f32[32,512]{1,0:T(8,128)S(1)} %fusion.41), channel_id=1, source_target_pairs={{0,4},{4,8},{8,12},{12,16},{16,20},{20,24},{24,28},{1,5},{5,9},{9,... | collective-permute-start | bytes 196616 | tf_op jit(solution)/shard_map/ppermute | solution.py:10
  55.2 1.9 %collective-permute-done.3 = f32[32,512]{1,0:T(8,128)S(1)} collective-permute-done((f32[32,512]{1,0:T(8,128)S(1)}, f32[32,512]{1,0:T(8,128)S(1)}, u32[]{:S(2)}, u32[]{:S(2)}) %collective-permute-start.3) | collective-permute-done | bytes 65568 | tf_op jit(solution)/shard_map/ppermute | solution.py:10
  57.5 5.2 %collective-permute-start.4 = (f32[32,512]{1,0:T(8,128)S(1)}, f32[32,512]{1,0:T(8,128)S(1)}, u32[]{:S(2)}, u32[]{:S(2)}) collective-permute-start(f32[32,512]{1,0:T(8,128)S(1)} %fusion.37), channel_id=1, source_target_pairs={{0,4},{4,8},{8,12},{12,16},{16,20},{20,24},{24,28},{1,5},{5,9},{9,... | collective-permute-start | bytes 196616 | tf_op jit(solution)/shard_map/ppermute | solution.py:10
  62.7 1.9 %collective-permute-done.4 = f32[32,512]{1,0:T(8,128)S(1)} collective-permute-done((f32[32,512]{1,0:T(8,128)S(1)}, f32[32,512]{1,0:T(8,128)S(1)}, u32[]{:S(2)}, u32[]{:S(2)}) %collective-permute-start.4) | collective-permute-done | bytes 65568 | tf_op jit(solution)/shard_map/ppermute | solution.py:10
  65.1 5.2 %collective-permute-start.5 = (f32[32,512]{1,0:T(8,128)S(1)}, f32[32,512]{1,0:T(8,128)S(1)}, u32[]{:S(2)}, u32[]{:S(2)}) collective-permute-start(f32[32,512]{1,0:T(8,128)S(1)} %fusion.33), channel_id=1, source_target_pairs={{0,4},{4,8},{8,12},{12,16},{16,20},{20,24},{24,28},{1,5},{5,9},{9,... | collective-permute-start | bytes 196616 | tf_op jit(solution)/shard_map/ppermute | solution.py:10
  70.2 1.9 %collective-permute-done.5 = f32[32,512]{1,0:T(8,128)S(1)} collective-permute-done((f32[32,512]{1,0:T(8,128)S(1)}, f32[32,512]{1,0:T(8,128)S(1)}, u32[]{:S(2)}, u32[]{:S(2)}) %collective-permute-start.5) | collective-permute-done | bytes 65568 | tf_op jit(solution)/shard_map/ppermute | solution.py:10
  73.2 1.3 collective-permute-start.7
  74.5 6.6 %collective-permute-done.7 = f32[32,512]{1,0:T(8,128)S(1)} collective-permute-done((f32[32,512]{1,0:T(8,128)S(1)}, f32[32,512]{1,0:T(8,128)S(1)}, u32[]{:S(2)}, u32[]{:S(2)}) %collective-permute-start.7) | collective-permute-done | bytes 65568 | tf_op jit(solution)/shard_map/ppermute | solution.py:10
  81.8 1.3 collective-permute-start.8
  83.1 5.7 %collective-permute-done.8 = f32[32,512]{1,0:T(8,128)S(1)} collective-permute-done((f32[32,512]{1,0:T(8,128)S(1)}, f32[32,512]{1,0:T(8,128)S(1)}, u32[]{:S(2)}, u32[]{:S(2)}) %collective-permute-start.8) | collective-permute-done | bytes 65568 | tf_op jit(solution)/shard_map/ppermute | solution.py:10
  89.4 1.3 collective-permute-start.9
  90.7 5.8 %collective-permute-done.9 = f32[32,512]{1,0:T(8,128)S(1)} collective-permute-done((f32[32,512]{1,0:T(8,128)S(1)}, f32[32,512]{1,0:T(8,128)S(1)}, u32[]{:S(2)}, u32[]{:S(2)}) %collective-permute-start.9) | collective-permute-done | bytes 65568 | tf_op jit(solution)/shard_map/ppermute | solution.py:10
  97.1 1.3 collective-permute-start.10
  98.4 5.8 %collective-permute-done.10 = f32[32,512]{1,0:T(8,128)S(1)} collective-permute-done((f32[32,512]{1,0:T(8,128)S(1)}, f32[32,512]{1,0:T(8,128)S(1)}, u32[]{:S(2)}, u32[]{:S(2)}) %collective-permute-start.10) | collective-permute-done | bytes 65568 | tf_op jit(solution)/shard_map/ppermute | solution.py:10
  104.8 1.3 collective-permute-start.11
  106.1 5.4 %collective-permute-start.6 = (f32[32,512]{1,0:T(8,128)S(1)}, f32[32,512]{1,0:T(8,128)S(1)}, u32[]{:S(2)}, u32[]{:S(2)}) collective-permute-start(f32[32,512]{1,0:T(8,128)S(1)} %get-tuple-element.82), channel_id=1, source_target_pairs={{0,4},{4,8},{8,12},{12,16},{16,20},{20,24},{24,28},{1,5},{5,9},{9,... | collective-permute-start | bytes 196616 | tf_op jit(solution)/shard_map/ppermute | solution.py:10
  112.5 1.3 collective-permute-start.12
  114.1 5.5 %collective-permute-done.12 = f32[32,512]{1,0:T(8,128)S(1)} collective-permute-done((f32[32,512]{1,0:T(8,128)S(1)}, f32[32,512]{1,0:T(8,128)S(1)}, u32[]{:S(2)}, u32[]{:S(2)}) %collective-permute-start.12) | collective-permute-done | bytes 65568 | tf_op jit(solution)/shard_map/ppermute | solution.py:10
  120.2 1.3 collective-permute-start.13
  121.7 5.5 %collective-permute-done.13 = f32[32,512]{1,0:T(8,128)S(1)} collective-permute-done((f32[32,512]{1,0:T(8,128)S(1)}, f32[32,512]{1,0:T(8,128)S(1)}, u32[]{:S(2)}, u32[]{:S(2)}) %collective-permute-start.13) | collective-permute-done | bytes 65568 | tf_op jit(solution)/shard_map/ppermute | solution.py:10
  129.7 8.4 %all_to_all.24 = f32[4,1,16384]{2,1,0:T(1,128)S(1)} all-to-all(f32[4,1,16384]{2,1,0:T(1,128)S(1)} %reshape.17), channel_id=1, replica_groups=mesh['tm'=8,'col'=4] {'col'}, dimensions={0} | all-to-all | bytes 524288 | tf_op jit(solution)/shard_map/all_to_all | solution.py:80
  138.6 1.4 reduce
  (107 shorter events, 18.0 us)
Async XLA Ops:
  7.2 0.8 copy-start
  7.2 21.9 %all-gather.2.cloned.1.call-start = ((), (), s32[]{:S(2)}) async-start(), calls=%async_computation.2 | async-start | bytes 1310720 | tf_op jit(solution)/shard_map/all_gather | solution.py:31
  8.7 11.7 %all-to-all-start = ((bf16[2,128,128]{2,0,1:T(2,128)(2,1)}), bf16[2,128,128]{2,0,1:T(2,128)(2,1)S(1)}, u32[]{:S(2)}, u32[]{:S(2)}) async-start(bf16[2,128,128]{2,0,1:T(2,128)(2,1)} %copy.10), calls=%async_computation | async-start | bytes 131072 | tf_op jit(solution)/shard_map/all_to_all | solution.py:36
  12.9 0.7 copy-start.2
  12.9 0.7 copy-start.3
  18.9 0.7 copy-start.1
  30.9 5.3 %collective-permute-start = (f32[32,512]{1,0:T(8,128)S(1)}, f32[32,512]{1,0:T(8,128)S(1)}, u32[]{:S(2)}, u32[]{:S(2)}) collective-permute-start(f32[32,512]{1,0:T(8,128)S(1)} %fusion.53), channel_id=1, source_target_pairs={{0,4},{4,8},{8,12},{12,16},{16,20},{20,24},{24,28},{1,5},{5,9},{9,... | collective-permute-start | bytes 196616 | tf_op jit(solution)/shard_map/ppermute | solution.py:10
  36.7 6.2 %collective-permute-start.1 = (f32[32,512]{1,0:T(8,128)S(1)}, f32[32,512]{1,0:T(8,128)S(1)}, u32[]{:S(2)}, u32[]{:S(2)}) collective-permute-start(f32[32,512]{1,0:T(8,128)S(1)} %fusion.49), channel_id=1, source_target_pairs={{0,4},{4,8},{8,12},{12,16},{16,20},{20,24},{24,28},{1,5},{5,9},{9,... | collective-permute-start | bytes 196616 | tf_op jit(solution)/shard_map/ppermute | solution.py:10
  43.3 6.2 %collective-permute-start.2 = (f32[32,512]{1,0:T(8,128)S(1)}, f32[32,512]{1,0:T(8,128)S(1)}, u32[]{:S(2)}, u32[]{:S(2)}) collective-permute-start(f32[32,512]{1,0:T(8,128)S(1)} %fusion.45), channel_id=1, source_target_pairs={{0,4},{4,8},{8,12},{12,16},{16,20},{20,24},{24,28},{1,5},{5,9},{9,... | collective-permute-start | bytes 196616 | tf_op jit(solution)/shard_map/ppermute | solution.py:10
  50.0 7.1 %collective-permute-start.3 = (f32[32,512]{1,0:T(8,128)S(1)}, f32[32,512]{1,0:T(8,128)S(1)}, u32[]{:S(2)}, u32[]{:S(2)}) collective-permute-start(f32[32,512]{1,0:T(8,128)S(1)} %fusion.41), channel_id=1, source_target_pairs={{0,4},{4,8},{8,12},{12,16},{16,20},{20,24},{24,28},{1,5},{5,9},{9,... | collective-permute-start | bytes 196616 | tf_op jit(solution)/shard_map/ppermute | solution.py:10
  57.5 7.1 %collective-permute-start.4 = (f32[32,512]{1,0:T(8,128)S(1)}, f32[32,512]{1,0:T(8,128)S(1)}, u32[]{:S(2)}, u32[]{:S(2)}) collective-permute-start(f32[32,512]{1,0:T(8,128)S(1)} %fusion.37), channel_id=1, source_target_pairs={{0,4},{4,8},{8,12},{12,16},{16,20},{20,24},{24,28},{1,5},{5,9},{9,... | collective-permute-start | bytes 196616 | tf_op jit(solution)/shard_map/ppermute | solution.py:10
  65.1 7.1 %collective-permute-start.5 = (f32[32,512]{1,0:T(8,128)S(1)}, f32[32,512]{1,0:T(8,128)S(1)}, u32[]{:S(2)}, u32[]{:S(2)}) collective-permute-start(f32[32,512]{1,0:T(8,128)S(1)} %fusion.33), channel_id=1, source_target_pairs={{0,4},{4,8},{8,12},{12,16},{16,20},{20,24},{24,28},{1,5},{5,9},{9,... | collective-permute-start | bytes 196616 | tf_op jit(solution)/shard_map/ppermute | solution.py:10
  73.2 7.9 %collective-permute-start.7 = (f32[32,512]{1,0:T(8,128)S(1)}, f32[32,512]{1,0:T(8,128)S(1)}, u32[]{:S(2)}, u32[]{:S(2)}) collective-permute-start(f32[32,512]{1,0:T(8,128)S(1)} %fusion.21), channel_id=1, source_target_pairs={{4,0},{8,4},{12,8},{16,12},{20,16},{24,20},{28,24},{5,1},{9,5},{13... | collective-permute-start | bytes 196616 | tf_op jit(solution)/shard_map/ppermute | solution.py:10
  81.8 7.0 %collective-permute-start.8 = (f32[32,512]{1,0:T(8,128)S(1)}, f32[32,512]{1,0:T(8,128)S(1)}, u32[]{:S(2)}, u32[]{:S(2)}) collective-permute-start(f32[32,512]{1,0:T(8,128)S(1)} %fusion.18), channel_id=1, source_target_pairs={{4,0},{8,4},{12,8},{16,12},{20,16},{24,20},{28,24},{5,1},{9,5},{13... | collective-permute-start | bytes 196616 | tf_op jit(solution)/shard_map/ppermute | solution.py:10
  89.4 7.1 %collective-permute-start.9 = (f32[32,512]{1,0:T(8,128)S(1)}, f32[32,512]{1,0:T(8,128)S(1)}, u32[]{:S(2)}, u32[]{:S(2)}) collective-permute-start(f32[32,512]{1,0:T(8,128)S(1)} %fusion.15), channel_id=1, source_target_pairs={{4,0},{8,4},{12,8},{16,12},{20,16},{24,20},{28,24},{5,1},{9,5},{13... | collective-permute-start | bytes 196616 | tf_op jit(solution)/shard_map/ppermute | solution.py:10
  97.1 7.1 %collective-permute-start.10 = (f32[32,512]{1,0:T(8,128)S(1)}, f32[32,512]{1,0:T(8,128)S(1)}, u32[]{:S(2)}, u32[]{:S(2)}) collective-permute-start(f32[32,512]{1,0:T(8,128)S(1)} %fusion.12), channel_id=1, source_target_pairs={{4,0},{8,4},{12,8},{16,12},{20,16},{24,20},{28,24},{5,1},{9,5},{13... | collective-permute-start | bytes 196616 | tf_op jit(solution)/shard_map/ppermute | solution.py:10
  104.8 7.1 %collective-permute-start.11 = (f32[32,512]{1,0:T(8,128)S(1)}, f32[32,512]{1,0:T(8,128)S(1)}, u32[]{:S(2)}, u32[]{:S(2)}) collective-permute-start(f32[32,512]{1,0:T(8,128)S(1)} %fusion.9), channel_id=1, source_target_pairs={{4,0},{8,4},{12,8},{16,12},{20,16},{24,20},{28,24},{5,1},{9,5},{13... | collective-permute-start | bytes 196616 | tf_op jit(solution)/shard_map/ppermute | solution.py:10
  106.1 7.9 %collective-permute-start.6 = (f32[32,512]{1,0:T(8,128)S(1)}, f32[32,512]{1,0:T(8,128)S(1)}, u32[]{:S(2)}, u32[]{:S(2)}) collective-permute-start(f32[32,512]{1,0:T(8,128)S(1)} %get-tuple-element.82), channel_id=1, source_target_pairs={{0,4},{4,8},{8,12},{12,16},{16,20},{20,24},{24,28},{1,5},{5,9},{9,... | collective-permute-start | bytes 196616 | tf_op jit(solution)/shard_map/ppermute | solution.py:10
  112.5 7.1 %collective-permute-start.12 = (f32[32,512]{1,0:T(8,128)S(1)}, f32[32,512]{1,0:T(8,128)S(1)}, u32[]{:S(2)}, u32[]{:S(2)}) collective-permute-start(f32[32,512]{1,0:T(8,128)S(1)} %fusion.6), channel_id=1, source_target_pairs={{4,0},{8,4},{12,8},{16,12},{20,16},{24,20},{28,24},{5,1},{9,5},{13... | collective-permute-start | bytes 196616 | tf_op jit(solution)/shard_map/ppermute | solution.py:10
  120.2 7.1 %collective-permute-start.13 = (f32[32,512]{1,0:T(8,128)S(1)}, f32[32,512]{1,0:T(8,128)S(1)}, u32[]{:S(2)}, u32[]{:S(2)}) collective-permute-start(f32[32,512]{1,0:T(8,128)S(1)} %fusion.3), channel_id=1, source_target_pairs={{4,0},{8,4},{12,8},{16,12},{20,16},{24,20},{28,24},{5,1},{9,5},{13... | collective-permute-start | bytes 196616 | tf_op jit(solution)/shard_map/ppermute | solution.py:10
Sparse Core Ops, SparseCore 0:
  9.5 19.5 all-gather.1
where the time goes:
time: 151 us; the launch traced here: 150 us
  waiting for transfers between devices  55.9 us (37%)
  starting transfers between devices  46.2 us (31%)
  between operations  14.6 us (10%)
  blocking collectives  13.7 us (9%)
  local copies, waits for them, and re-layouts  8.34 us (6%)
  matrix products  7.36 us (5%)
  other arithmetic  3.76 us (2%)
    ppermute x14, waiting for transfers between devices, passed_along(): return lax.ppermute(shard, axis, pairs)  46.7 us
    ppermute x14, starting transfers between devices, passed_along(): return lax.ppermute(shard, axis, pairs)  41.9 us
    all_gather x1, waiting for transfers between devices, local(): full_coupling = lax.all_gather(coupling, 'col', axis=2, tiled=True)  8.51 us
    all_to_all x1, blocking collectives, local(): both = lax.all_to_all(both, 'col', split_axis=3, concat_axis=2, tiled=True)  8.39 us
    dot_general x31, matrix products, split_dot(): lax.dot_general(both, weights, (((1,), (contract,)), ((), ())), preferred...  7.36 us
    all_gather x1, blocking collectives, local(): small = lax.all_gather(small, 'col', axis=1, tiled=True)  5.29 us
    all_to_all x1, starting transfers between devices, local(): lax.all_to_all(observed, 'col', split_axis=1, concat_axis=2, tiled=True)  4.24 us
    unnamed x11, local copies, waits for them, and re-layouts  4.14 us
  transfers between devices with their start and end apart: 16, of which 15 were waited for; matrix products, arithmetic and copies ran while one was open for 2% of the time, Pallas kernels for 0%

commit v1 on v0

--- a/solution.py
+++ b/solution.py
@@ -28,7 +28,18 @@
     block_count = pattern.shape[0]
     block_size = state_width // block_count
     time_groups = lax.axis_size("tm")
-    full_coupling = lax.all_gather(coupling, "col", axis=2, tiled=True)
+    m = coupling
+    reached = lax.axis_size("col")
+    built = lax.axis_index("col")
+    v_next, v1, outer = (reached, built, m.shape[2])
+    rack = [s * v_next if hop_no == 2 else s for hop_no, s in enumerate(m.shape)]
+    f_now = jnp.zeros(rack, m.dtype)
+    full_coupling = lax.dynamic_update_slice_in_dim(f_now, m, v1 * outer, axis=2)
+    for no in range(1, v_next):
+        m = lax.ppermute(m, "col", [(hop_no, (hop_no + 1) % v_next) for hop_no in range(v_next)])
+        full_coupling = lax.dynamic_update_slice_in_dim(
+            full_coupling, m, (v1 - no) % v_next * outer, axis=2
+        )
     small = jnp.concatenate([persist, input_gain[None]], axis=0)
     small = lax.all_gather(small, "col", axis=1, tiled=True)
     diag = small[:step_count]

time: 151 us -> 140 us (0.927)
  between operations: 14.6 us -> 1.33 us
  local copies, waits for them, and re-layouts: 8.34 us -> 10.3 us
    ppermute x0 -> x3, waiting for transfers between devices: none -> 8.51 us  [local(): lax.ppermute(m, 'col', [(hop_no, (hop_no + 1) % v_next) for hop_no in ran...]
    all_gather x1 -> x0, waiting for transfers between devices: 8.51 us -> none  [local(): full_coupling = lax.all_gather(coupling, 'col', axis=2, tiled=True)]
    unnamed x11, local copies, waits for them, and re-layouts: 4.14 us -> 5.75 us
  transfers between devices with their start and end apart: 16 -> 18, of which waited for: 15 -> 15; matrix products, arithmetic and copies ran while one was open for 2% -> 3% of each run, Pallas kernels for 0% -> 0%
where the time goes in v1:
time: 140 us; the launch traced here: 139 us
  waiting for transfers between devices  55.3 us (40%)
  starting transfers between devices  46.9 us (34%)
  blocking collectives  15.1 us (11%)
  local copies, waits for them, and re-layouts  10.3 us (7%)
  matrix products  7.33 us (5%)
  other arithmetic  2.53 us (2%)
    ppermute x14, waiting for transfers between devices, passed_along(): return lax.ppermute(shard, axis, pairs)  46.8 us
    ppermute x14, starting transfers between devices, passed_along(): return lax.ppermute(shard, axis, pairs)  42.3 us
    all_to_all x1, blocking collectives, local(): both = lax.all_to_all(both, 'col', split_axis=3, concat_axis=2, tiled=True)  9.18 us
    ppermute x3, waiting for transfers between devices, local(): lax.ppermute(m, 'col', [(hop_no, (hop_no + 1) % v_next) for hop_no in ran...  8.51 us
    dot_general x31, matrix products, split_dot(): lax.dot_general(both, weights, (((1,), (contract,)), ((), ())), preferred...  7.33 us
    all_gather x1, blocking collectives, local(): small = lax.all_gather(small, 'col', axis=1, tiled=True)  5.89 us
    unnamed x11, local copies, waits for them, and re-layouts  5.75 us
    all_to_all x1, starting transfers between devices, local(): lax.all_to_all(observed, 'col', split_axis=1, concat_axis=2, tiled=True)  3.86 us
  transfers between devices with their start and end apart: 18, of which 15 were waited for; matrix products, arithmetic and copies ran while one was open for 3% of the time, Pallas kernels for 0%

profile of v1, /device:TPU:0, one launch (start us, length us, event | category | flops | bytes accessed | tf_op | source)
XLA Modules:
  0.0 138.8 jit_solution(16682823817032455229)
XLA Ops:
  1.2 1.5 %copy.10 = bf16[2,128,128]{2,0,1:T(2,128)(2,1)} copy(bf16[2,128,128]{2,1,0:T(8,128)(2,1)} %param.5) | data formatting | bytes 131072 | tf_op args[0]
  2.7 3.9 %all-to-all-start = ((bf16[2,128,128]{2,0,1:T(2,128)(2,1)}), bf16[2,128,128]{2,0,1:T(2,128)(2,1)S(1)}, u32[]{:S(2)}, u32[]{:S(2)}) async-start(bf16[2,128,128]{2,0,1:T(2,128)(2,1)} %copy.10), calls=%async_computation | async-start | bytes 131072 | tf_op jit(solution)/shard_map/all_to_all | solution.py:47
  7.3 5.9 %all_gather.3 = f32[3,512]{1,0:T(4,128)S(1)} all-gather(f32[3,128]{1,0:T(4,128)S(1)} %pad_maximum_fusion.1), channel_id=1, replica_groups=mesh['tm'=8,'col'=4] {'col'}, dimensions={1}, use_global_device_ids=true | all-gather | bytes 7680 | tf_op jit(solution)/shard_map/all_gather | solution.py:44
  16.1 2.9 %collective-permute-done.1 = bf16[2,512,128]{2,1,0:T(8,128)(2,1)S(1)} collective-permute-done((bf16[2,512,128]{2,1,0:T(8,128)(2,1)S(1)}, bf16[2,512,128]{2,1,0:T(8,128)(2,1)S(1)}, u32[]{:S(2)}, u32[]{:S(2)}) %collective-permute-start.1) | collective-permute-done | bytes 262176 | tf_op jit(solution)/shard_map/ppermute | solution.py:39
  19.2 5.6 %collective-permute-done.2 = bf16[2,512,128]{2,1,0:T(8,128)(2,1)S(1)} collective-permute-done((bf16[2,512,128]{2,1,0:T(8,128)(2,1)S(1)}, bf16[2,512,128]{2,1,0:T(8,128)(2,1)S(1)}, u32[]{:S(2)}, u32[]{:S(2)}) %collective-permute-start.2) | collective-permute-done | bytes 262176 | tf_op jit(solution)/shard_map/ppermute | solution.py:39
  25.5 3.4 %collective-permute-start.3 = (f32[32,512]{1,0:T(8,128)S(1)}, f32[32,512]{1,0:T(8,128)S(1)}, u32[]{:S(2)}, u32[]{:S(2)}) collective-permute-start(f32[32,512]{1,0:T(8,128)S(1)} %fusion.53), channel_id=1, source_target_pairs={{0,4},{4,8},{8,12},{12,16},{16,20},{20,24},{24,28},{1,5},{5,9},{9,... | collective-permute-start | bytes 196616 | tf_op jit(solution)/shard_map/ppermute | solution.py:10
  28.9 1.9 %collective-permute-done.3 = f32[32,512]{1,0:T(8,128)S(1)} collective-permute-done((f32[32,512]{1,0:T(8,128)S(1)}, f32[32,512]{1,0:T(8,128)S(1)}, u32[]{:S(2)}, u32[]{:S(2)}) %collective-permute-start.3) | collective-permute-done | bytes 65568 | tf_op jit(solution)/shard_map/ppermute | solution.py:10
  31.3 4.3 %collective-permute-start.4 = (f32[32,512]{1,0:T(8,128)S(1)}, f32[32,512]{1,0:T(8,128)S(1)}, u32[]{:S(2)}, u32[]{:S(2)}) collective-permute-start(f32[32,512]{1,0:T(8,128)S(1)} %fusion.49), channel_id=1, source_target_pairs={{0,4},{4,8},{8,12},{12,16},{16,20},{20,24},{24,28},{1,5},{5,9},{9,... | collective-permute-start | bytes 196616 | tf_op jit(solution)/shard_map/ppermute | solution.py:10
  35.5 1.9 %collective-permute-done.4 = f32[32,512]{1,0:T(8,128)S(1)} collective-permute-done((f32[32,512]{1,0:T(8,128)S(1)}, f32[32,512]{1,0:T(8,128)S(1)}, u32[]{:S(2)}, u32[]{:S(2)}) %collective-permute-start.4) | collective-permute-done | bytes 65568 | tf_op jit(solution)/shard_map/ppermute | solution.py:10
  37.9 4.3 %collective-permute-start.5 = (f32[32,512]{1,0:T(8,128)S(1)}, f32[32,512]{1,0:T(8,128)S(1)}, u32[]{:S(2)}, u32[]{:S(2)}) collective-permute-start(f32[32,512]{1,0:T(8,128)S(1)} %fusion.45), channel_id=1, source_target_pairs={{0,4},{4,8},{8,12},{12,16},{16,20},{20,24},{24,28},{1,5},{5,9},{9,... | collective-permute-start | bytes 196616 | tf_op jit(solution)/shard_map/ppermute | solution.py:10
  42.2 1.9 %collective-permute-done.5 = f32[32,512]{1,0:T(8,128)S(1)} collective-permute-done((f32[32,512]{1,0:T(8,128)S(1)}, f32[32,512]{1,0:T(8,128)S(1)}, u32[]{:S(2)}, u32[]{:S(2)}) %collective-permute-start.5) | collective-permute-done | bytes 65568 | tf_op jit(solution)/shard_map/ppermute | solution.py:10
  44.6 5.2 %collective-permute-start.6 = (f32[32,512]{1,0:T(8,128)S(1)}, f32[32,512]{1,0:T(8,128)S(1)}, u32[]{:S(2)}, u32[]{:S(2)}) collective-permute-start(f32[32,512]{1,0:T(8,128)S(1)} %fusion.41), channel_id=1, source_target_pairs={{0,4},{4,8},{8,12},{12,16},{16,20},{20,24},{24,28},{1,5},{5,9},{9,... | collective-permute-start | bytes 196616 | tf_op jit(solution)/shard_map/ppermute | solution.py:10
  49.8 1.9 %collective-permute-done.6 = f32[32,512]{1,0:T(8,128)S(1)} collective-permute-done((f32[32,512]{1,0:T(8,128)S(1)}, f32[32,512]{1,0:T(8,128)S(1)}, u32[]{:S(2)}, u32[]{:S(2)}) %collective-permute-start.6) | collective-permute-done | bytes 65568 | tf_op jit(solution)/shard_map/ppermute | solution.py:10
  52.2 5.2 %collective-permute-start.7 = (f32[32,512]{1,0:T(8,128)S(1)}, f32[32,512]{1,0:T(8,128)S(1)}, u32[]{:S(2)}, u32[]{:S(2)}) collective-permute-start(f32[32,512]{1,0:T(8,128)S(1)} %fusion.37), channel_id=1, source_target_pairs={{0,4},{4,8},{8,12},{12,16},{16,20},{20,24},{24,28},{1,5},{5,9},{9,... | collective-permute-start | bytes 196616 | tf_op jit(solution)/shard_map/ppermute | solution.py:10
  57.3 2.0 %collective-permute-done.7 = f32[32,512]{1,0:T(8,128)S(1)} collective-permute-done((f32[32,512]{1,0:T(8,128)S(1)}, f32[32,512]{1,0:T(8,128)S(1)}, u32[]{:S(2)}, u32[]{:S(2)}) %collective-permute-start.7) | collective-permute-done | bytes 65568 | tf_op jit(solution)/shard_map/ppermute | solution.py:10
  59.8 5.5 %collective-permute-start.8 = (f32[32,512]{1,0:T(8,128)S(1)}, f32[32,512]{1,0:T(8,128)S(1)}, u32[]{:S(2)}, u32[]{:S(2)}) collective-permute-start(f32[32,512]{1,0:T(8,128)S(1)} %fusion.33), channel_id=1, source_target_pairs={{0,4},{4,8},{8,12},{12,16},{16,20},{20,24},{24,28},{1,5},{5,9},{9,... | collective-permute-start | bytes 196616 | tf_op jit(solution)/shard_map/ppermute | solution.py:10
  65.3 1.9 %collective-permute-done.8 = f32[32,512]{1,0:T(8,128)S(1)} collective-permute-done((f32[32,512]{1,0:T(8,128)S(1)}, f32[32,512]{1,0:T(8,128)S(1)}, u32[]{:S(2)}, u32[]{:S(2)}) %collective-permute-start.8) | collective-permute-done | bytes 65568 | tf_op jit(solution)/shard_map/ppermute | solution.py:10
  68.3 1.3 collective-permute-start.10
  69.6 6.2 %collective-permute-done.10 = f32[32,512]{1,0:T(8,128)S(1)} collective-permute-done((f32[32,512]{1,0:T(8,128)S(1)}, f32[32,512]{1,0:T(8,128)S(1)}, u32[]{:S(2)}, u32[]{:S(2)}) %collective-permute-start.10) | collective-permute-done | bytes 65568 | tf_op jit(solution)/shard_map/ppermute | solution.py:10
  76.4 1.3 collective-permute-start.11
  77.7 6.1 %collective-permute-done.11 = f32[32,512]{1,0:T(8,128)S(1)} collective-permute-done((f32[32,512]{1,0:T(8,128)S(1)}, f32[32,512]{1,0:T(8,128)S(1)}, u32[]{:S(2)}, u32[]{:S(2)}) %collective-permute-start.11) | collective-permute-done | bytes 65568 | tf_op jit(solution)/shard_map/ppermute | solution.py:10
  84.5 1.3 collective-permute-start.12
  85.8 5.8 %collective-permute-done.12 = f32[32,512]{1,0:T(8,128)S(1)} collective-permute-done((f32[32,512]{1,0:T(8,128)S(1)}, f32[32,512]{1,0:T(8,128)S(1)}, u32[]{:S(2)}, u32[]{:S(2)}) %collective-permute-start.12) | collective-permute-done | bytes 65568 | tf_op jit(solution)/shard_map/ppermute | solution.py:10
  92.2 1.3 collective-permute-start.13
  93.5 5.8 %collective-permute-done.13 = f32[32,512]{1,0:T(8,128)S(1)} collective-permute-done((f32[32,512]{1,0:T(8,128)S(1)}, f32[32,512]{1,0:T(8,128)S(1)}, u32[]{:S(2)}, u32[]{:S(2)}) %collective-permute-start.13) | collective-permute-done | bytes 65568 | tf_op jit(solution)/shard_map/ppermute | solution.py:10
  99.9 1.3 collective-permute-start.14
  101.2 5.4 %collective-permute-start.9 = (f32[32,512]{1,0:T(8,128)S(1)}, f32[32,512]{1,0:T(8,128)S(1)}, u32[]{:S(2)}, u32[]{:S(2)}) collective-permute-start(f32[32,512]{1,0:T(8,128)S(1)} %get-tuple-element.82), channel_id=1, source_target_pairs={{0,4},{4,8},{8,12},{12,16},{16,20},{20,24},{24,28},{1,5},{5,9},{9,... | collective-permute-start | bytes 196616 | tf_op jit(solution)/shard_map/ppermute | solution.py:10
  107.6 1.3 collective-permute-start.15
  108.9 5.7 %collective-permute-done.15 = f32[32,512]{1,0:T(8,128)S(1)} collective-permute-done((f32[32,512]{1,0:T(8,128)S(1)}, f32[32,512]{1,0:T(8,128)S(1)}, u32[]{:S(2)}, u32[]{:S(2)}) %collective-permute-start.15) | collective-permute-done | bytes 65568 | tf_op jit(solution)/shard_map/ppermute | solution.py:10
  116.8 5.5 %collective-permute-done.16 = f32[32,512]{1,0:T(8,128)S(1)} collective-permute-done((f32[32,512]{1,0:T(8,128)S(1)}, f32[32,512]{1,0:T(8,128)S(1)}, u32[]{:S(2)}, u32[]{:S(2)}) %collective-permute-start.16) | collective-permute-done | bytes 65568 | tf_op jit(solution)/shard_map/ppermute | solution.py:10
  124.7 9.2 %all_to_all.24 = f32[4,1,16384]{2,1,0:T(1,128)S(1)} all-to-all(f32[4,1,16384]{2,1,0:T(1,128)S(1)} %reshape.17), channel_id=1, replica_groups=mesh['tm'=8,'col'=4] {'col'}, dimensions={0} | all-to-all | bytes 524288 | tf_op jit(solution)/shard_map/all_to_all | solution.py:91
  134.4 1.4 reduce
  (115 shorter events, 19.6 us)
Async XLA Ops:
  0.6 12.5 %collective-permute-start = (bf16[2,512,128]{2,1,0:T(8,128)(2,1)}, bf16[2,512,128]{2,1,0:T(8,128)(2,1)S(1)}, u32[]{:S(2)}, u32[]{:S(2)}) collective-permute-start(bf16[2,512,128]{2,1,0:T(8,128)(2,1)} %param.8), channel_id=1, source_target_pairs={{0,1},{1,2},{2,3},{3,0},{4,5},{5,6},{6,7},{7,4},{8,9},{9,10},{10,1... | collective-permute-start | bytes 786440 | tf_op jit(solution)/shard_map/ppermute | solution.py:39
  2.7 13.3 %all-to-all-start = ((bf16[2,128,128]{2,0,1:T(2,128)(2,1)}), bf16[2,128,128]{2,0,1:T(2,128)(2,1)S(1)}, u32[]{:S(2)}, u32[]{:S(2)}) async-start(bf16[2,128,128]{2,0,1:T(2,128)(2,1)} %copy.10), calls=%async_computation | async-start | bytes 131072 | tf_op jit(solution)/shard_map/all_to_all | solution.py:47
  6.6 0.7 copy-start.2
  6.6 0.7 copy-start.3
  13.2 5.8 %collective-permute-start.1 = (bf16[2,512,128]{2,1,0:T(8,128)(2,1)S(1)}, bf16[2,512,128]{2,1,0:T(8,128)(2,1)S(1)}, u32[]{:S(2)}, u32[]{:S(2)}) collective-permute-start(bf16[2,512,128]{2,1,0:T(8,128)(2,1)S(1)} %collective-permute-done), channel_id=1, source_target_pairs={{0,1},{1,2},{2,3},{3,0},{4,5},{5,6},{6,7},{7,4},{8,9},{9,10},{10,1... | collective-permute-start | bytes 786440 | tf_op jit(solution)/shard_map/ppermute | solution.py:39
  13.4 0.9 copy-start
  14.5 0.7 copy-start.1
  19.0 5.8 %collective-permute-start.2 = (bf16[2,512,128]{2,1,0:T(8,128)(2,1)S(1)}, bf16[2,512,128]{2,1,0:T(8,128)(2,1)S(1)}, u32[]{:S(2)}, u32[]{:S(2)}) collective-permute-start(bf16[2,512,128]{2,1,0:T(8,128)(2,1)S(1)} %collective-permute-done.1), channel_id=1, source_target_pairs={{0,1},{1,2},{2,3},{3,0},{4,5},{5,6},{6,7},{7,4},{8,9},{9,10},{10,1... | collective-permute-start | bytes 786440 | tf_op jit(solution)/shard_map/ppermute | solution.py:39
  25.5 5.3 %collective-permute-start.3 = (f32[32,512]{1,0:T(8,128)S(1)}, f32[32,512]{1,0:T(8,128)S(1)}, u32[]{:S(2)}, u32[]{:S(2)}) collective-permute-start(f32[32,512]{1,0:T(8,128)S(1)} %fusion.53), channel_id=1, source_target_pairs={{0,4},{4,8},{8,12},{12,16},{16,20},{20,24},{24,28},{1,5},{5,9},{9,... | collective-permute-start | bytes 196616 | tf_op jit(solution)/shard_map/ppermute | solution.py:10
  31.3 6.2 %collective-permute-start.4 = (f32[32,512]{1,0:T(8,128)S(1)}, f32[32,512]{1,0:T(8,128)S(1)}, u32[]{:S(2)}, u32[]{:S(2)}) collective-permute-start(f32[32,512]{1,0:T(8,128)S(1)} %fusion.49), channel_id=1, source_target_pairs={{0,4},{4,8},{8,12},{12,16},{16,20},{20,24},{24,28},{1,5},{5,9},{9,... | collective-permute-start | bytes 196616 | tf_op jit(solution)/shard_map/ppermute | solution.py:10
  37.9 6.2 %collective-permute-start.5 = (f32[32,512]{1,0:T(8,128)S(1)}, f32[32,512]{1,0:T(8,128)S(1)}, u32[]{:S(2)}, u32[]{:S(2)}) collective-permute-start(f32[32,512]{1,0:T(8,128)S(1)} %fusion.45), channel_id=1, source_target_pairs={{0,4},{4,8},{8,12},{12,16},{16,20},{20,24},{24,28},{1,5},{5,9},{9,... | collective-permute-start | bytes 196616 | tf_op jit(solution)/shard_map/ppermute | solution.py:10
  44.6 7.1 %collective-permute-start.6 = (f32[32,512]{1,0:T(8,128)S(1)}, f32[32,512]{1,0:T(8,128)S(1)}, u32[]{:S(2)}, u32[]{:S(2)}) collective-permute-start(f32[32,512]{1,0:T(8,128)S(1)} %fusion.41), channel_id=1, source_target_pairs={{0,4},{4,8},{8,12},{12,16},{16,20},{20,24},{24,28},{1,5},{5,9},{9,... | collective-permute-start | bytes 196616 | tf_op jit(solution)/shard_map/ppermute | solution.py:10
  52.2 7.2 %collective-permute-start.7 = (f32[32,512]{1,0:T(8,128)S(1)}, f32[32,512]{1,0:T(8,128)S(1)}, u32[]{:S(2)}, u32[]{:S(2)}) collective-permute-start(f32[32,512]{1,0:T(8,128)S(1)} %fusion.37), channel_id=1, source_target_pairs={{0,4},{4,8},{8,12},{12,16},{16,20},{20,24},{24,28},{1,5},{5,9},{9,... | collective-permute-start | bytes 196616 | tf_op jit(solution)/shard_map/ppermute | solution.py:10
  59.8 7.4 %collective-permute-start.8 = (f32[32,512]{1,0:T(8,128)S(1)}, f32[32,512]{1,0:T(8,128)S(1)}, u32[]{:S(2)}, u32[]{:S(2)}) collective-permute-start(f32[32,512]{1,0:T(8,128)S(1)} %fusion.33), channel_id=1, source_target_pairs={{0,4},{4,8},{8,12},{12,16},{16,20},{20,24},{24,28},{1,5},{5,9},{9,... | collective-permute-start | bytes 196616 | tf_op jit(solution)/shard_map/ppermute | solution.py:10
  68.3 7.5 %collective-permute-start.10 = (f32[32,512]{1,0:T(8,128)S(1)}, f32[32,512]{1,0:T(8,128)S(1)}, u32[]{:S(2)}, u32[]{:S(2)}) collective-permute-start(f32[32,512]{1,0:T(8,128)S(1)} %fusion.21), channel_id=1, source_target_pairs={{4,0},{8,4},{12,8},{16,12},{20,16},{24,20},{28,24},{5,1},{9,5},{13... | collective-permute-start | bytes 196616 | tf_op jit(solution)/shard_map/ppermute | solution.py:10
  76.4 7.4 %collective-permute-start.11 = (f32[32,512]{1,0:T(8,128)S(1)}, f32[32,512]{1,0:T(8,128)S(1)}, u32[]{:S(2)}, u32[]{:S(2)}) collective-permute-start(f32[32,512]{1,0:T(8,128)S(1)} %fusion.18), channel_id=1, source_target_pairs={{4,0},{8,4},{12,8},{16,12},{20,16},{24,20},{28,24},{5,1},{9,5},{13... | collective-permute-start | bytes 196616 | tf_op jit(solution)/shard_map/ppermute | solution.py:10
  84.5 7.1 %collective-permute-start.12 = (f32[32,512]{1,0:T(8,128)S(1)}, f32[32,512]{1,0:T(8,128)S(1)}, u32[]{:S(2)}, u32[]{:S(2)}) collective-permute-start(f32[32,512]{1,0:T(8,128)S(1)} %fusion.15), channel_id=1, source_target_pairs={{4,0},{8,4},{12,8},{16,12},{20,16},{24,20},{28,24},{5,1},{9,5},{13... | collective-permute-start | bytes 196616 | tf_op jit(solution)/shard_map/ppermute | solution.py:10
  92.2 7.1 %collective-permute-start.13 = (f32[32,512]{1,0:T(8,128)S(1)}, f32[32,512]{1,0:T(8,128)S(1)}, u32[]{:S(2)}, u32[]{:S(2)}) collective-permute-start(f32[32,512]{1,0:T(8,128)S(1)} %fusion.12), channel_id=1, source_target_pairs={{4,0},{8,4},{12,8},{16,12},{20,16},{24,20},{28,24},{5,1},{9,5},{13... | collective-permute-start | bytes 196616 | tf_op jit(solution)/shard_map/ppermute | solution.py:10
  99.9 7.1 %collective-permute-start.14 = (f32[32,512]{1,0:T(8,128)S(1)}, f32[32,512]{1,0:T(8,128)S(1)}, u32[]{:S(2)}, u32[]{:S(2)}) collective-permute-start(f32[32,512]{1,0:T(8,128)S(1)} %fusion.9), channel_id=1, source_target_pairs={{4,0},{8,4},{12,8},{16,12},{20,16},{24,20},{28,24},{5,1},{9,5},{13... | collective-permute-start | bytes 196616 | tf_op jit(solution)/shard_map/ppermute | solution.py:10
  101.2 7.7 %collective-permute-start.9 = (f32[32,512]{1,0:T(8,128)S(1)}, f32[32,512]{1,0:T(8,128)S(1)}, u32[]{:S(2)}, u32[]{:S(2)}) collective-permute-start(f32[32,512]{1,0:T(8,128)S(1)} %get-tuple-element.82), channel_id=1, source_target_pairs={{0,4},{4,8},{8,12},{12,16},{16,20},{20,24},{24,28},{1,5},{5,9},{9,... | collective-permute-start | bytes 196616 | tf_op jit(solution)/shard_map/ppermute | solution.py:10
  107.6 7.1 %collective-permute-start.15 = (f32[32,512]{1,0:T(8,128)S(1)}, f32[32,512]{1,0:T(8,128)S(1)}, u32[]{:S(2)}, u32[]{:S(2)}) collective-permute-start(f32[32,512]{1,0:T(8,128)S(1)} %fusion.6), channel_id=1, source_target_pairs={{4,0},{8,4},{12,8},{16,12},{20,16},{24,20},{28,24},{5,1},{9,5},{13... | collective-permute-start | bytes 196616 | tf_op jit(solution)/shard_map/ppermute | solution.py:10
  115.3 7.1 %collective-permute-start.16 = (f32[32,512]{1,0:T(8,128)S(1)}, f32[32,512]{1,0:T(8,128)S(1)}, u32[]{:S(2)}, u32[]{:S(2)}) collective-permute-start(f32[32,512]{1,0:T(8,128)S(1)} %fusion.3), channel_id=1, source_target_pairs={{4,0},{8,4},{12,8},{16,12},{20,16},{24,20},{28,24},{5,1},{9,5},{13... | collective-permute-start | bytes 196616 | tf_op jit(solution)/shard_map/ppermute | solution.py:10
